TPU v7x, 128 devices: a whole 4x4x4 slice. The times are simulated.
128 devices in a mesh: dp: 32 (over y, z_lo, x), tensor: 4 (over z_hi, core).
Axes of the slice: x: 4, y: 4, z: 4 (z_hi: 2, z_lo: 2; z = z_hi * 2 + z_lo), core: 2. Of those that a mesh axis runs over, the one named last changes fastest.
Arguments:
- tokens: bfloat16 [32768, 4096], P('dp'), may hold values from -6 to 6
- grad_out: bfloat16 [32768, 2048], P('dp', 'tensor'), may hold values from -12 to 12
- w_query: bfloat16 [4096, 2048], P('dp', 'tensor'), may hold values from -2 to 2
- w_key: bfloat16 [4096, 512], P('dp', 'tensor'), may hold values from -2 to 2
- value_matrix: bfloat16 [4096, 512], P('dp', 'tensor'), may hold values from -0.09375 to 0.09375
Outputs:
- grad_tokens: bfloat16 [32768, 4096], P('dp', 'tensor')
- grad_query: bfloat16 [4096, 2048], P('dp', 'tensor')
- grad_key: bfloat16 [4096, 512], P('dp', 'tensor')
- grad_value: bfloat16 [4096, 512], P('dp', 'tensor')
All inputs are finite; a program needn't handle non-finite values.
Results may differ from a plain program's by a relative error of at most 0.03.
The roundings to bfloat16 on the way count: a program that leaves them out, or rounds other values in their place, can miss the bound.
Values may be sent and summed in bfloat16 or wider, within the bound.
No kernel may reach another device: no remote copies, remote signals or barrier semaphores. Data moves between devices by JAX's collectives and lax.ppermute only.
A program may use at most 192 MiB of HBM per device.

v0:
```python
import jax
import jax.numpy as jnp
from jax import lax
from jax.sharding import PartitionSpec as P

MODEL_WIDTH = 4096
HEAD_SIZE = 128
rope_base = 500000.0


def position_tables(length, head_dim):
    half_dim = head_dim // 2
    positions = jnp.arange(length, dtype=jnp.float32)
    inverse = jnp.power(
        jnp.float32(rope_base), -2.0 * jnp.arange(half_dim, dtype=jnp.float32) / head_dim
    )
    angles = positions[:, None] * inverse[None, :]
    cosine = jnp.concatenate([jnp.cos(angles), jnp.cos(angles)], axis=-1)[:, None, :]
    sine_table = jnp.concatenate([jnp.sin(angles), jnp.sin(angles)], axis=-1)[:, None, :]
    return (cosine, sine_table)


def half_turn(values):
    lower, upper = jnp.split(values, 2, axis=-1)
    return jnp.concatenate([-upper, lower], axis=-1)


def rotate_forward(values, cosine, sine_table):
    return values * cosine + half_turn(values) * sine_table


def rotate_back(grads, cosine, sine_table):
    return grads * cosine - half_turn(grads * sine_table)


def attention_backward(unrotated_query, unrotated_key, projected_value, upstream_flat, kv_heads):
    length = unrotated_query.shape[0]
    heads = unrotated_query.shape[1] // HEAD_SIZE
    group_size = heads // kv_heads
    cosine, sine_table = position_tables(length, HEAD_SIZE)
    query = rotate_forward(
        unrotated_query.reshape(length, heads, HEAD_SIZE), cosine, sine_table
    ).astype(jnp.bfloat16)
    key = rotate_forward(
        unrotated_key.reshape(length, kv_heads, HEAD_SIZE), cosine, sine_table
    ).astype(jnp.bfloat16)
    value = projected_value.reshape(length, kv_heads, HEAD_SIZE).astype(jnp.bfloat16)
    query_grouped = query.reshape(length, kv_heads, group_size, HEAD_SIZE)
    upstream = upstream_flat.reshape(length, kv_heads, group_size, HEAD_SIZE)
    scale = 1.0 / jnp.sqrt(jnp.float32(HEAD_SIZE))
    scores = (
        jnp.einsum("ikgd,jkd->kgij", query_grouped, key, preferred_element_type=jnp.float32) * scale
    )
    positions = jnp.arange(length, dtype=jnp.int32)
    causal = positions[:, None] >= positions[None, :]
    scores = jnp.where(causal, scores, -jnp.inf)
    row_max = jnp.max(scores, axis=-1, keepdims=True)
    weights = jnp.exp(scores - row_max)
    weights = weights / jnp.sum(weights, axis=-1, keepdims=True)
    weights_b = weights.astype(jnp.bfloat16)
    dprob = jnp.einsum("ikgd,jkd->kgij", upstream, value, preferred_element_type=jnp.float32)
    rowdot = jnp.sum(weights * dprob, axis=-1, keepdims=True)
    dscore = (weights * (dprob - rowdot) * scale).astype(jnp.bfloat16)
    dquery = jnp.einsum("kgij,jkd->ikgd", dscore, key, preferred_element_type=jnp.float32).reshape(
        length, heads, HEAD_SIZE
    )
    dkey = jnp.einsum("kgij,ikgd->jkd", dscore, query_grouped, preferred_element_type=jnp.float32)
    dvalue = jnp.einsum("kgij,ikgd->jkd", weights_b, upstream, preferred_element_type=jnp.float32)
    query_gradient = (
        rotate_back(dquery, cosine, sine_table)
        .astype(jnp.bfloat16)
        .reshape(length, heads * HEAD_SIZE)
    )
    key_gradient = (
        rotate_back(dkey, cosine, sine_table)
        .astype(jnp.bfloat16)
        .reshape(length, kv_heads * HEAD_SIZE)
    )
    value_gradient = dvalue.astype(jnp.bfloat16).reshape(length, kv_heads * HEAD_SIZE)
    return (query_gradient, key_gradient, value_gradient)


def contract_cols(grads, weight_rows):
    return lax.dot_general(
        grads, weight_rows, (((1,), (1,)), ((), ())), preferred_element_type=jnp.float32
    )


def body(tokens, grad_out, w_query, w_key, value_matrix):
    query_cols = w_query.shape[1]
    key_value_columns = w_key.shape[1]
    kv_dev = key_value_columns // HEAD_SIZE
    pieces = (
        lax.all_gather(w_query, "dp", axis=0, tiled=True),
        lax.all_gather(w_key, "dp", axis=0, tiled=True),
        lax.all_gather(value_matrix, "dp", axis=0, tiled=True),
    )
    unrotated_query, unrotated_key, projected_value = tuple(
        (jnp.dot(tokens, piece, preferred_element_type=jnp.float32) for piece in pieces)
    )
    query_gradient, key_gradient, value_gradient = attention_backward(
        unrotated_query, unrotated_key, projected_value, grad_out, kv_dev
    )
    combined = jnp.concatenate([query_gradient, key_gradient, value_gradient], axis=1)
    pieces = lax.all_gather((w_query, w_key, value_matrix), "dp", axis=0, tiled=True)
    partial_sum = (
        contract_cols(query_gradient, pieces[0])
        + contract_cols(key_gradient, pieces[1])
        + contract_cols(value_gradient, pieces[2])
    )
    summed_all = lax.psum(partial_sum.astype(jnp.bfloat16), "tensor").astype(jnp.float32)
    share_width = MODEL_WIDTH // lax.axis_size("tensor")
    grad_tokens = lax.dynamic_slice_in_dim(
        summed_all, lax.axis_index("tensor") * share_width, share_width, 1
    )
    grads_all = lax.psum_scatter(
        lax.dot_general(
            tokens, combined, (((0,), (0,)), ((), ())), preferred_element_type=jnp.float32
        ).astype(jnp.bfloat16),
        "dp",
        scatter_dimension=0,
        tiled=True,
    ).astype(jnp.float32)
    grad_query = grads_all[:, :query_cols].astype(jnp.bfloat16)
    grad_key = grads_all[:, query_cols : query_cols + key_value_columns].astype(jnp.bfloat16)
    grad_value = grads_all[:, query_cols + key_value_columns :].astype(jnp.bfloat16)
    return (grad_tokens.astype(jnp.bfloat16), grad_query, grad_key, grad_value)


def solution(mesh):
    in_specs = (
        P("dp", None),
        P("dp", "tensor"),
        P("dp", "tensor"),
        P("dp", "tensor"),
        P("dp", "tensor"),
    )
    out_specs = (P("dp", "tensor"), P("dp", "tensor"), P("dp", "tensor"), P("dp", "tensor"))
    return jax.shard_map(body, mesh=mesh, in_specs=in_specs, out_specs=out_specs, check_vma=False)
```

profile of v0, /device:TPU:0, one launch (start us, length us, event | category | flops | bytes accessed | tf_op | source)
XLA Modules:
  0.0 889.6 jit_solution(15293957988102845399)
XLA Ops:
  7.2 0.0 all-gather.4.cloned.1.call-start
  7.2 0.7 all-gather.4.cloned.1.call-update
  7.9 0.0 all-gather.6.cloned.1.call-start
  7.9 0.7 all-gather.6.cloned.1.call-update
  8.6 0.0 all-gather.8.cloned.1.call-start
  8.7 0.7 all-gather.8.cloned.1.call-update
  9.4 0.0 all-reduce.2.cloned.1.call-start
  9.4 0.3 iota_compare_fusion
  9.8 1.0 fusion.38
  10.8 0.0 copy-start.10
  10.8 2.4 copy.40
  13.1 149.9 %all-gather.4.cloned.1.call-done = bf16[4096,128]{1,0:T(8,128)(2,1)} async-done(((bf16[128,128]{1,0:T(8,128)(2,1)}), bf16[4096,128]{1,0:T(8,128)(2,1)}) %all-gather.4.cloned.1.call-update) | async-done | bytes 1048592 | tf_op jit(solution)/shard_map/all_gather | solution.py:95
  163.1 6.5 fusion.43
  169.6 1.2 pad_maximum_fusion.1
  170.8 151.1 %all-gather.6.cloned.1.call-done = bf16[4096,512]{1,0:T(8,128)(2,1)} async-done(((bf16[128,512]{1,0:T(8,128)(2,1)}), bf16[4096,512]{1,0:T(8,128)(2,1)}) %all-gather.6.cloned.1.call-update) | async-done | bytes 4194320 | tf_op jit(solution)/shard_map/all_gather | solution.py:94
  321.9 8.3 fusion.44
  330.2 0.2 slice_negate_fusion.1
  330.4 0.2 maximum_multiply_fusion
  330.6 0.0 copy-start.1
  330.6 0.6 copy-done.3
  331.2 0.6 fusion.14
  331.8 0.1 copy-done.1
  331.9 3.1 fusion.6
  335.1 3.6 fusion.5
  338.7 2.3 copy-done
  341.0 6.0 fusion.25
  347.0 127.4 %all-gather.8.cloned.1.call-done = bf16[4096,128]{1,0:T(8,128)(2,1)} async-done(((bf16[128,128]{1,0:T(8,128)(2,1)}), bf16[4096,128]{1,0:T(8,128)(2,1)}) %all-gather.8.cloned.1.call-update) | async-done | bytes 1048592 | tf_op jit(solution)/shard_map/all_gather | solution.py:96
  474.4 18.2 %fusion = (f32[4,1024]{1,0:T(4,128)S(1)}, f32[1024,1024,4]{1,0,2:T(8,128)}) fusion(f32[4,1024]{1,0:T(4,128)S(1)} %fusion.5, f32[4,1024]{1,0:T(4,128)S(1)} %get-tuple-element.27, f32[1024,1024,4]{1,0,2:T(8,128)} %copy-done, pred[1024,1024]{0,1:T(8,128)(4,1)S(1)} %iota_compare_fusion, bf16[1024,4,128]{0,2,1:T(8,128)(2,1)} %bitcast.132, ...), kind=kOutput, calls=%fused_computation.3 | convolution fusion | flops 2172776448 | bytes 45137920 | tf_op jit(solution)/shard_map/ikgd,jkd->kgij/dot_general | solution.py:61
  492.7 13.4 %fusion.7 = bf16[4,1024,1024]{1,2,0:T(8,128)(2,1)S(1)} fusion(f32[1024,1024,4]{1,0,2:T(8,128)} %get-tuple-element.30, f32[4,1024]{1,0:T(4,128)S(1)} %get-tuple-element.29, f32[4,1024]{1,0:T(4,128)S(1)} %fusion.5, f32[4,1024]{1,0:T(4,128)S(1)} %get-tuple-element.27, f32[1024,1024,4]{1,0,2:T(8,128)} %copy-done, pred[1024,1024]{0,1:T(8,128)(4,1)S(1)} %iota_compare_fusion), kind=kLoop, calls=%fused_computation.12 | loop fusion | flops 33554432 | bytes 43040768 | tf_op jit(solution)/shard_map/reshape.19
  506.1 3.0 bitcast_multiply_fusion.4
  509.1 1.4 bitcast_multiply_fusion.3
  510.5 0.3 slice_negate_fusion
  510.8 0.2 pad_maximum_fusion
  511.0 0.6 fusion.16
  511.7 0.1 fusion.34
  511.8 8.1 fusion.46
  519.9 8.1 fusion.45
  528.0 15.3 %add_convert_fusion = bf16[1024,4096]{1,0:T(8,128)(2,1)} fusion(f32[1024,4096]{1,0:T(8,128)} %fusion.45, f32[1024,4096]{1,0:T(8,128)} %fusion.46, bf16[1024,128]{0,1:T(8,128)(2,1)S(1)} %copy-done.14, bf16[4096,128]{1,0:T(8,128)(2,1)S(1)} %copy-done.13), kind=kOutput, calls=%fused_computation.7 | convolution fusion | flops 1086324736 | bytes 43253760 | tf_op jit(solution)/shard_map/dot_general | solution.py:84
  543.4 0.0 all-reduce.2.cloned.1.call-update
  543.4 0.0 reduce-scatter.4.cloned.1.call-start
  543.4 13.3 %fusion.11 = bf16[4096,768]{0,1:T(8,128)(2,1)} fusion(bf16[1024,4096]{1,0:T(8,128)(2,1)} %param.5, bf16[1024,128]{0,1:T(8,128)(2,1)S(1)} %copy-done.14, bf16[1024,128]{0,1:T(8,128)(2,1)S(1)} %fusion.34, bf16[1024,512]{0,1:T(8,128)(2,1)S(1)} %fusion.16), kind=kOutput, calls=%fused_computation.17 | convolution fusion | flops 6450315264 | bytes 16252928 | tf_op jit(solution)/shard_map/dot_general | solution.py:117
  556.7 8.5 copy.35
  565.2 0.0 reduce-scatter.4.cloned.1.call-update
  565.2 138.8 %all-reduce.2.cloned.1.call-done = bf16[1024,4096]{1,0:T(8,128)(2,1)} async-done(((bf16[1024,4096]{1,0:T(8,128)(2,1)}), bf16[1024,4096]{1,0:T(8,128)(2,1)}) %all-reduce.2.cloned.1.call-update) | async-done | bytes 8388624 | tf_op jit(solution)/shard_map/psum | solution.py:111
  704.0 3.1 convert_convert_fusion
  707.1 173.1 %reduce-scatter.4.cloned.1.call-done = bf16[128,768]{1,0:T(8,128)(2,1)} async-done(((bf16[4096,768]{1,0:T(8,128)(2,1)}), bf16[128,768]{1,0:T(8,128)(2,1)}) %reduce-scatter.4.cloned.1.call-update) | async-done | bytes 196624
  880.1 1.6 slice.15
  881.7 1.4 fusion.42
  (30 shorter events, 0.1 us)
Async XLA Ops:
  7.2 155.9 %all-gather.4.cloned.1.call-start = ((), (), s32[]{:S(2)}) async-start(), calls=%async_computation.1 | async-start | bytes 1081344 | tf_op jit(solution)/shard_map/all_gather | solution.py:95
  7.9 314.0 %all-gather.6.cloned.1.call-start = ((), (), s32[]{:S(2)}) async-start(), calls=%async_computation.2 | async-start | bytes 4325376 | tf_op jit(solution)/shard_map/all_gather | solution.py:94
  8.6 465.8 %all-gather.8.cloned.1.call-start = ((), (), s32[]{:S(2)}) async-start(), calls=%async_computation.3 | async-start | bytes 1081344 | tf_op jit(solution)/shard_map/all_gather | solution.py:96
  9.4 694.6 %all-reduce.2.cloned.1.call-start = ((), (), s32[]{:S(2)}) async-start(), calls=%async_computation.4 | async-start | bytes 16777216 | tf_op jit(solution)/shard_map/psum | solution.py:111
  10.8 158.9 %copy-start.10 = (f32[1024,64]{0,1:T(8,128)}, f32[1024,64]{0,1:T(8,128)S(1)}, u32[]{:S(2)}) copy-start(f32[1024,64]{0,1:T(8,128)S(1)} %get-tuple-element.25) | copy-start | bytes 786436
  321.9 8.5 copy-start.5
  330.2 1.0 copy-start.3
  330.2 1.7 copy-start.8
  330.6 1.3 copy-start.1
  335.0 5.9 copy-start
  335.1 5.9 copy-start.12
  492.6 13.4 %copy-start.2 = (f32[1024,4,128]{0,2,1:T(8,128)S(1)}, f32[1024,4,128]{0,2,1:T(8,128)}, u32[]{:S(2)}) copy-start(f32[1024,4,128]{0,2,1:T(8,128)} %copy-done.1) | copy-start | bytes 6291460
  492.7 13.4 %copy-start.4 = (f32[1024,128]{0,1:T(8,128)S(1)}, f32[1024,128]{0,1:T(8,128)}, u32[]{:S(2)}) copy-start(f32[1024,128]{0,1:T(8,128)} %get-tuple-element.20) | copy-start | bytes 1572868
  506.1 3.0 copy-start.6
  506.1 3.0 copy-start.9
  510.5 1.2 copy-start.11
  510.5 1.3 copy-start.7
  511.8 8.1 copy-start.15
  519.9 8.1 copy-start.13
  519.9 8.1 copy-start.14
  543.4 336.8 %reduce-scatter.4.cloned.1.call-start = ((), (), s32[]{:S(2)}) async-start(), calls=%async_computation.5 | async-start | bytes 6488064
Sparse Core Ops, SparseCore 0:
  9.6 153.3 all-gather.3
  164.7 157.1 all-gather.5
  323.5 150.8 all-gather.7
  543.5 160.4 all-reduce.1
  706.3 173.8 reduce-scatter.3
where the time goes:
time: 890 us
  waiting for transfers between devices  742 us (83%)
  matrix products  91.3 us (10%)
  other arithmetic  24.8 us (3%)
  local copies, waits for them, and re-layouts  16.8 us (2%)
  between operations  14.1 us (2%)
    unnamed x6, waiting for transfers between devices  175 us
    all_gather x1, waiting for transfers between devices, body(): lax.all_gather(w_query, 'dp', axis=0, tiled=True)  151 us
    all_gather x1, waiting for transfers between devices, body(): lax.all_gather(w_key, 'dp', axis=0, tiled=True)  150 us
    psum x1, waiting for transfers between devices, body(): lax.psum(partial_sum.astype(jnp.bfloat16), 'tensor').astype(jnp.float32)  139 us
    all_gather x1, waiting for transfers between devices, body(): lax.all_gather(value_matrix, 'dp', axis=0, tiled=True)  127 us
    dot_general x3, matrix products, contract_cols(): lax.dot_general(grads, weight_rows, (((1,), (1,)), ((), ())), preferred_e...  31.5 us
    dot_general x1, matrix products, attention_backward(): jnp.einsum('ikgd,jkd->kgij', upstream, value, preferred_element_type=jnp....  18.2 us
  transfers between devices with their start and end apart: 5, of which 5 were waited for; matrix products, arithmetic and copies ran while one was open for 7% of the time, Pallas kernels for 0%

commit v1 on v0

--- a/solution.py
+++ b/solution.py
@@ -108,7 +108,9 @@
         + contract_cols(key_gradient, pieces[1])
         + contract_cols(value_gradient, pieces[2])
     )
-    summed_all = lax.psum(partial_sum.astype(jnp.bfloat16), "tensor").astype(jnp.float32)
+    summed_all = jnp.sum(lax.all_gather(partial_sum.astype(jnp.bfloat16), "tensor"), axis=0).astype(
+        jnp.float32
+    )
     share_width = MODEL_WIDTH // lax.axis_size("tensor")
     grad_tokens = lax.dynamic_slice_in_dim(
         summed_all, lax.axis_index("tensor") * share_width, share_width, 1

time: 890 us -> 937 us (1.053)
  waiting for transfers between devices: 742 us -> 774 us
  other arithmetic: 24.8 us -> 41.2 us
    all_gather x0 -> x1, waiting for transfers between devices: none -> 201 us  [body(): lax.all_gather(partial_sum.astype(jnp.bfloat16), 'tensor')]
    psum x1 -> x0, waiting for transfers between devices: 139 us -> none  [body(): lax.psum(partial_sum.astype(jnp.bfloat16), 'tensor').astype(jnp.float32)]
    unnamed x6, waiting for transfers between devices: 175 us -> 145 us
    reduce_sum x0 -> x1, other arithmetic: none -> 16.4 us  [body(): jnp.sum(lax.all_gather(partial_sum.astype(jnp.bfloat16), 'tensor'), axis=0)]
where the time goes in v1:
time: 937 us; the launch traced here: 936 us
  waiting for transfers between devices  774 us (83%)
  matrix products  86.9 us (9%)
  other arithmetic  41.2 us (4%)
  local copies, waits for them, and re-layouts  19.5 us (2%)
  between operations  14.1 us (2%)
    all_gather x1, waiting for transfers between devices, body(): lax.all_gather(partial_sum.astype(jnp.bfloat16), 'tensor')  201 us
    all_gather x1, waiting for transfers between devices, body(): lax.all_gather(w_query, 'dp', axis=0, tiled=True)  151 us
    all_gather x1, waiting for transfers between devices, body(): lax.all_gather(w_key, 'dp', axis=0, tiled=True)  150 us
    unnamed x6, waiting for transfers between devices  145 us
    all_gather x1, waiting for transfers between devices, body(): lax.all_gather(value_matrix, 'dp', axis=0, tiled=True)  127 us
    dot_general x3, matrix products, contract_cols(): lax.dot_general(grads, weight_rows, (((1,), (1,)), ((), ())), preferred_e...  31.7 us
  transfers between devices with their start and end apart: 5, of which 5 were waited for; matrix products, arithmetic and copies ran while one was open for 7% of the time, Pallas kernels for 0%

profile of v1, /device:TPU:0, one launch (start us, length us, event | category | flops | bytes accessed | tf_op | source)
XLA Modules:
  0.0 935.7 jit_solution(9260135792116241314)
XLA Ops:
  7.2 0.0 all-gather.6.cloned.1.call-start
  7.2 0.7 all-gather.6.cloned.1.call-update
  7.9 0.0 all-gather.8.cloned.1.call-start
  7.9 0.7 all-gather.8.cloned.1.call-update
  8.6 0.0 all-gather.10.cloned.1.call-start
  8.7 0.7 all-gather.10.cloned.1.call-update
  9.4 0.0 reduce-scatter.4.cloned.1.call-start
  9.4 0.3 iota_compare_fusion
  9.8 1.0 fusion.38
  10.8 2.4 copy.40
  13.1 149.9 %all-gather.6.cloned.1.call-done = bf16[4096,128]{1,0:T(8,128)(2,1)} async-done(((bf16[128,128]{1,0:T(8,128)(2,1)}), bf16[4096,128]{1,0:T(8,128)(2,1)}) %all-gather.6.cloned.1.call-update) | async-done | bytes 1048592 | tf_op jit(solution)/shard_map/all_gather | solution.py:95
  163.1 6.5 fusion.43
  169.6 1.2 pad_maximum_fusion.1
  170.8 151.1 %all-gather.8.cloned.1.call-done = bf16[4096,512]{1,0:T(8,128)(2,1)} async-done(((bf16[128,512]{1,0:T(8,128)(2,1)}), bf16[4096,512]{1,0:T(8,128)(2,1)}) %all-gather.8.cloned.1.call-update) | async-done | bytes 4194320 | tf_op jit(solution)/shard_map/all_gather | solution.py:94
  321.9 8.3 fusion.44
  330.2 0.2 slice_negate_fusion.1
  330.4 0.2 maximum_multiply_fusion
  330.6 0.6 copy-done.3
  331.2 0.6 fusion.14
  331.8 0.1 copy-done.1
  331.9 3.1 fusion.6
  335.1 3.6 fusion.5
  338.7 2.3 copy-done
  341.0 6.0 fusion.25
  347.0 127.4 %all-gather.10.cloned.1.call-done = bf16[4096,128]{1,0:T(8,128)(2,1)} async-done(((bf16[128,128]{1,0:T(8,128)(2,1)}), bf16[4096,128]{1,0:T(8,128)(2,1)}) %all-gather.10.cloned.1.call-update) | async-done | bytes 1048592 | tf_op jit(solution)/shard_map/all_gather | solution.py:96
  474.4 18.2 %fusion = (f32[4,1024]{1,0:T(4,128)S(1)}, f32[1024,1024,4]{1,0,2:T(8,128)}) fusion(f32[4,1024]{1,0:T(4,128)S(1)} %fusion.5, f32[4,1024]{1,0:T(4,128)S(1)} %get-tuple-element.27, f32[1024,1024,4]{1,0,2:T(8,128)} %copy-done, pred[1024,1024]{0,1:T(8,128)(4,1)S(1)} %iota_compare_fusion, bf16[1024,4,128]{0,2,1:T(8,128)(2,1)} %bitcast.136, ...), kind=kOutput, calls=%fused_computation.3 | convolution fusion | flops 2172776448 | bytes 45137920 | tf_op jit(solution)/shard_map/ikgd,jkd->kgij/dot_general | solution.py:61
  492.7 13.4 %fusion.7 = bf16[4,1024,1024]{1,2,0:T(8,128)(2,1)S(1)} fusion(f32[1024,1024,4]{1,0,2:T(8,128)} %get-tuple-element.30, f32[4,1024]{1,0:T(4,128)S(1)} %get-tuple-element.29, f32[4,1024]{1,0:T(4,128)S(1)} %fusion.5, f32[4,1024]{1,0:T(4,128)S(1)} %get-tuple-element.27, f32[1024,1024,4]{1,0,2:T(8,128)} %copy-done, pred[1024,1024]{0,1:T(8,128)(4,1)S(1)} %iota_compare_fusion), kind=kLoop, calls=%fused_computation.12 | loop fusion | flops 33554432 | bytes 43040768 | tf_op jit(solution)/shard_map/reshape.19
  506.1 3.0 bitcast_multiply_fusion.4
  509.1 1.4 bitcast_multiply_fusion.3
  510.5 0.3 slice_negate_fusion
  510.8 0.2 pad_maximum_fusion
  511.1 0.6 fusion.16
  511.7 0.1 fusion.34
  511.8 0.9 slice-done
  512.8 1.4 slice-done.1
  514.2 8.6 fusion.11
  522.8 8.7 copy.35
  531.5 0.0 reduce-scatter.4.cloned.1.call-update
  531.5 0.0 all-gather.12.cloned.1.call-start
  531.6 8.1 fusion.46
  539.7 8.1 fusion.45
  547.8 15.5 %add_convert_fusion = bf16[1024,4096]{1,0:T(8,128)(2,1)} fusion(f32[1024,4096]{1,0:T(8,128)} %fusion.45, f32[1024,4096]{1,0:T(8,128)} %fusion.46, bf16[1024,128]{0,1:T(8,128)(2,1)S(1)} %copy-done.14, bf16[4096,128]{1,0:T(8,128)(2,1)S(1)} %copy-done.13), kind=kOutput, calls=%fused_computation.7 | convolution fusion | flops 1086324736 | bytes 43253760 | tf_op jit(solution)/shard_map/dot_general | solution.py:84
  563.3 142.7 %reduce-scatter.4.cloned.1.call-done = bf16[128,768]{1,0:T(8,128)(2,1)} async-done(((bf16[4096,768]{1,0:T(8,128)(2,1)}), bf16[128,768]{1,0:T(8,128)(2,1)}) %reduce-scatter.4.cloned.1.call-update) | async-done | bytes 196624
  706.1 1.6 slice.15
  707.6 1.4 fusion.42
  709.0 200.7 %all-gather.12.cloned.1.call-done = bf16[4096,4096]{1,0:T(8,128)(2,1)} async-done(((bf16[1024,4096]{1,0:T(8,128)(2,1)}), bf16[4096,4096]{1,0:T(8,128)(2,1)}) %all-gather.12.cloned.1.call-update) | async-done | bytes 33554448 | tf_op jit(solution)/shard_map/all_gather | solution.py:111
  909.8 16.4 %reduce_sum.32 = bf16[1024,4096]{1,0:T(8,128)(2,1)} reduce(bf16[4,1024,4096]{2,1,0:T(8,128)(2,1)} %bitcast.129, bf16[]{:T(256)} %constant.8.clone.1), dimensions={0}, to_apply=%region_3.4 | reduce | flops 12582912 | bytes 41943040 | tf_op jit(solution)/shard_map/reduce_sum | solution.py:111
  926.1 3.1 convert_convert_fusion
  (36 shorter events, 0.2 us)
Async XLA Ops:
  7.2 155.9 %all-gather.6.cloned.1.call-start = ((), (), s32[]{:S(2)}) async-start(), calls=%async_computation.1 | async-start | bytes 1081344 | tf_op jit(solution)/shard_map/all_gather | solution.py:95
  7.9 314.0 %all-gather.8.cloned.1.call-start = ((), (), s32[]{:S(2)}) async-start(), calls=%async_computation.2 | async-start | bytes 4325376 | tf_op jit(solution)/shard_map/all_gather | solution.py:94
  8.6 465.8 %all-gather.10.cloned.1.call-start = ((), (), s32[]{:S(2)}) async-start(), calls=%async_computation.3 | async-start | bytes 1081344 | tf_op jit(solution)/shard_map/all_gather | solution.py:96
  9.4 696.7 %reduce-scatter.4.cloned.1.call-start = ((), (), s32[]{:S(2)}) async-start(), calls=%async_computation.5 | async-start | bytes 6488064
  10.8 158.9 %copy-start.10 = (f32[1024,64]{0,1:T(8,128)}, f32[1024,64]{0,1:T(8,128)S(1)}, u32[]{:S(2)}) copy-start(f32[1024,64]{0,1:T(8,128)S(1)} %get-tuple-element.25) | copy-start | bytes 786436
  321.9 8.5 copy-start.5
  330.2 1.0 copy-start.3
  330.2 1.7 copy-start.8
  330.6 1.3 copy-start.1
  335.0 5.9 copy-start
  335.1 5.9 copy-start.12
  492.6 13.4 %copy-start.2 = (f32[1024,4,128]{0,2,1:T(8,128)S(1)}, f32[1024,4,128]{0,2,1:T(8,128)}, u32[]{:S(2)}) copy-start(f32[1024,4,128]{0,2,1:T(8,128)} %copy-done.1) | copy-start | bytes 6291460
  492.6 13.4 %copy-start.4 = (f32[1024,128]{0,1:T(8,128)S(1)}, f32[1024,128]{0,1:T(8,128)}, u32[]{:S(2)}) copy-start(f32[1024,128]{0,1:T(8,128)} %get-tuple-element.20) | copy-start | bytes 1572868
  506.1 3.0 copy-start.6
  506.1 3.0 copy-start.9
  510.5 1.2 copy-start.11
  510.5 2.3 slice-start
  510.5 2.3 copy-start.14
  510.8 3.4 slice-start.1
  522.8 8.8 copy-start.7
  531.5 378.3 %all-gather.12.cloned.1.call-start = ((), (), s32[]{:S(2)}) async-start(), calls=%async_computation.4 | async-start | bytes 41943040 | tf_op jit(solution)/shard_map/all_gather | solution.py:111
  531.6 8.1 copy-start.15
  539.7 8.1 copy-start.13
Sparse Core Ops, SparseCore 0:
  9.6 153.3 all-gather.5
  164.7 157.1 all-gather.7
  323.5 150.8 all-gather.9
  531.6 174.3 reduce-scatter.3
  707.6 202.1 all-gather.11
